TPU v7x, 32 devices: a whole 2x2x4 slice. The times are simulated.
32 devices in a mesh: day: 8 (over z, x), pt: 4 (over y, core).
Axes of the slice: x: 2, y: 2, z: 4, core: 2. Of those that a mesh axis runs over, the one named last changes fastest.
Arguments:
- points: bfloat16 [8, 64, 2048], P('day', None, 'pt'), may hold values from -0.45 to 0.45
- cells: bfloat16 [8, 64, 8192], P('day', None, 'pt'), may hold values from -0.44921875 to 0.44921875
- clone_weight: float32 [8, 64, 2048], P('day', None, 'pt'), may hold values from 0.1 to 1
- potential: float32 [8, 2048], P('day', 'pt'), may hold values from 0.2 to 5
- support_count: int32 [8], P('day'), may hold values from 512 to 2048, as said below
- cell_count: int32 [8], P('day'), may hold values from 2048 to 8192, as said below
Outputs:
- forward_message: float32 [8, 64, 2048], P('day', None, 'pt')
- backward_message: float32 [8, 64, 2048], P('day', None, 'pt')
- fit_ratio: float32 [8, 2048], P('day', 'pt')
Inputs may be any that keep to these rules, and one draw needn't show every extreme that they name: Live support points of a day are its first support_count slots; some day has all 2048 slots live and some day has 512. Observed cells of a day are its first cell_count slots; some day fills all 8192 slots and some day has 2048.
All inputs are finite; a program needn't handle non-finite values.
Results may differ from a plain program's by a relative error of at most 0.0003.
Values may be sent and summed in bfloat16 or wider, within the bound.
No kernel may reach another device: no remote copies, remote signals or barrier semaphores. Data moves between devices by JAX's collectives and lax.ppermute only.
A program may use at most 64 MiB of HBM per device.

v0:
```python
import jax
import jax.numpy as jnp
from jax import lax
from jax.sharding import PartitionSpec as P


def with_halo(cells, sides, width):
    for axis, dim in sides:
        count = lax.axis_size(axis)
        ends = count - 1
        head = lax.slice_in_dim(cells, 0, width, axis=dim)
        tail = lax.slice_in_dim(cells, cells.shape[dim] - width, cells.shape[dim], axis=dim)
        cells = jnp.concatenate(
            [
                lax.ppermute(tail, axis, [(i, (i + 1) % count) for i in range(ends)]),
                cells,
                lax.ppermute(head, axis, [((i + 1) % count, i) for i in range(ends)]),
            ],
            axis=dim,
        )
    return cells


def shifted(block, axis, distance):
    devices = range(lax.axis_size(axis))
    route = [(i - distance, i) for i in devices if i - distance in devices]
    return lax.ppermute(block, axis, route)


def norm_of(coords):
    wide = coords.astype(jnp.float32)
    return jnp.sum(wide * wide, axis=0)


def squared_dist(left_pts, left_norm, right_pts, right_norm):
    inner = lax.dot_general(
        left_pts, right_pts, (((0,), (0,)), ((), ())), preferred_element_type=jnp.float32
    )
    return left_norm[:, None] + right_norm[None, :] - 2.0 * inner


def shards(points, cells, clone_weight, potential, support_count, cell_count):
    pt_rank = lax.axis_index("pt")
    day_index = lax.axis_index("day")
    day_count = lax.axis_size("day")
    full_pts, full_clone, full_pot = (
        lax.all_gather(points.astype(jnp.float32), "pt", axis=2, tiled=True).astype(points.dtype),
        lax.all_gather(clone_weight, "pt", axis=2, tiled=True),
        lax.all_gather(potential, "pt", axis=1, tiled=True),
    )
    beside_all = with_halo(full_pts, (("day", 0),), 1)
    before_day = beside_all[0]
    after_day = beside_all[2]
    own_pts = points[0]
    per_device = own_pts.shape[1]
    support_total = full_pts.shape[2]
    clones = clone_weight.shape[1]
    weight = full_clone[0] * full_pot
    live_total = support_count[0].astype(jnp.float32)
    live_all = (jnp.arange(support_total, dtype=jnp.int32) < support_count[0]).astype(jnp.float32)
    live_own = lax.dynamic_slice_in_dim(live_all, pt_rank * per_device, per_device)
    own_norm = norm_of(own_pts)
    before_norm = norm_of(before_day)
    after_norm = norm_of(after_day)
    row_span = 512
    span_count = support_total // row_span

    def kernel_rows(source_pts, source_norm, block_index):
        offset = block_index * row_span
        source_rows = lax.dynamic_slice_in_dim(source_pts, offset, row_span, 1)
        norm_rows = lax.dynamic_slice_in_dim(source_norm, offset, row_span, 0)
        return jnp.exp(-squared_dist(source_rows, norm_rows, own_pts, own_norm)).astype(
            jnp.bfloat16
        )

    def contract(sent_rows, source_pts, source_norm):

        def add_rows(block_index, result):
            sent_part = lax.dynamic_slice_in_dim(sent_rows, block_index * row_span, row_span, 1)
            return result + jnp.dot(
                sent_part,
                kernel_rows(source_pts, source_norm, block_index),
                preferred_element_type=jnp.float32,
            )

        return lax.fori_loop(
            0, span_count, add_rows, jnp.zeros((sent_rows.shape[0], per_device), jnp.float32)
        )

    block_count = 4
    block_rows = clones // block_count
    steps_total = day_count + block_count - 1
    empty_rows = jnp.zeros((block_rows, per_device), jnp.float32)
    seed_rows = jnp.broadcast_to(live_own[None, :], (block_rows, per_device))

    def settle(piece_rows, full_rows, valid):
        column_sums = jnp.sum(full_rows * live_all[None, :], axis=1, keepdims=True)
        column_sums = jnp.where(valid, column_sums, 1.0)
        own_part = piece_rows * live_own[None, :] * live_total / column_sums
        whole_part = full_rows * live_all[None, :] * live_total / column_sums
        return (own_part, whole_part)

    def one_step(step_index, carried):
        forward_in, backward_in, forward_out, backward_out = carried
        forward_at = step_index - day_index
        forward_ok = (forward_at >= 0) & (forward_at < block_count)
        forward_block = jnp.clip(forward_at, 0, block_count - 1)
        backward_at = step_index - (day_count - 1 - day_index)
        backward_ok = (backward_at >= 0) & (backward_at < block_count)
        backward_block = jnp.clip(backward_at, 0, block_count - 1)
        forward_got = lax.cond(
            forward_ok & (day_index > 0),
            lambda: contract(forward_in, before_day, before_norm),
            lambda: empty_rows,
        )
        forward_piece = jnp.where(day_index == 0, seed_rows, forward_got)
        backward_got = lax.cond(
            backward_ok & (day_index < day_count - 1),
            lambda: contract(backward_in, after_day, after_norm),
            lambda: empty_rows,
        )
        backward_piece = jnp.where(day_index == day_count - 1, seed_rows, backward_got)
        forward_full, backward_full = (
            lax.all_gather(forward_piece, "pt", axis=1, tiled=True),
            lax.all_gather(backward_piece, "pt", axis=1, tiled=True),
        )
        forward_own, forward_all = settle(forward_piece, forward_full, forward_ok)
        backward_own, backward_all = settle(backward_piece, backward_full, backward_ok)
        forward_out = jnp.where(
            forward_ok,
            lax.dynamic_update_slice_in_dim(
                forward_out, forward_own, forward_block * block_rows, 0
            ),
            forward_out,
        )
        backward_out = jnp.where(
            backward_ok,
            lax.dynamic_update_slice_in_dim(
                backward_out, backward_own, backward_block * block_rows, 0
            ),
            backward_out,
        )
        forward_sent = (
            forward_all
            * lax.dynamic_slice_in_dim(weight, forward_block * block_rows, block_rows, 0)
        ).astype(jnp.bfloat16)
        backward_sent = (
            backward_all
            * lax.dynamic_slice_in_dim(weight, backward_block * block_rows, block_rows, 0)
        ).astype(jnp.bfloat16)
        forward_in = shifted(forward_sent, "day", 1)
        backward_in = shifted(backward_sent, "day", -1)
        return (forward_in, backward_in, forward_out, backward_out)

    start_in = jnp.zeros((block_rows, support_total), jnp.bfloat16)
    start_out = jnp.zeros((clones, per_device), jnp.float32)
    carried = lax.fori_loop(0, steps_total, one_step, (start_in, start_in, start_out, start_out))
    forward_out = carried[2]
    backward_out = carried[3]
    mass_own = (
        live_own * potential[0] * jnp.sum(forward_out * clone_weight[0] * backward_out, axis=0)
    )
    cell_total = cell_count[0]
    cell_total_f = cell_total.astype(jnp.float32)
    full_mass = lax.all_gather(mass_own, "pt", axis=0, tiled=True)
    mass_total = jnp.sum(full_mass)
    own_cells = cells[0]
    cell_norm = norm_of(own_cells)
    own_slots = own_cells.shape[1]
    day_pts = full_pts[0]
    day_norm = norm_of(day_pts)
    fit_span = 256
    fit_blocks = support_total // fit_span

    def fit_rows(block_index):
        offset = block_index * fit_span
        chosen = lax.dynamic_slice_in_dim(day_pts, offset, fit_span, 1)
        chosen_norm = lax.dynamic_slice_in_dim(day_norm, offset, fit_span, 0)
        return jnp.exp(-squared_dist(chosen, chosen_norm, own_cells, cell_norm))

    def density_part(block_index):
        chosen_mass = lax.dynamic_slice_in_dim(full_mass, block_index * fit_span, fit_span, 0)
        return jnp.dot(chosen_mass, fit_rows(block_index), precision=lax.Precision.HIGHEST)

    density = jnp.sum(lax.map(density_part, jnp.arange(fit_blocks)), axis=0) / mass_total
    cell_live = (pt_rank * own_slots + jnp.arange(own_slots, dtype=jnp.int32) < cell_total).astype(
        jnp.float32
    )
    inverse = cell_live / density

    def ratio_part(block_index):
        return jnp.dot(fit_rows(block_index), inverse, precision=lax.Precision.HIGHEST)

    ratio_rows = lax.map(ratio_part, jnp.arange(fit_blocks)).reshape(support_total)
    summed = lax.psum_scatter(ratio_rows, "pt", scatter_dimension=0, tiled=True)
    fit_rows_out = live_own / cell_total_f * summed
    return (forward_out[None], backward_out[None], fit_rows_out[None])


def solution(mesh):
    in_specs = (
        P("day", None, "pt"),
        P("day", None, "pt"),
        P("day", None, "pt"),
        P("day", "pt"),
        P("day"),
        P("day"),
    )
    out_specs = (P("day", None, "pt"), P("day", None, "pt"), P("day", "pt"))
    return jax.shard_map(shards, mesh=mesh, in_specs=in_specs, out_specs=out_specs, check_vma=False)
```

profile of v0, /device:TPU:0, one launch (start us, length us, event | category | flops | bytes accessed | tf_op | source)
XLA Modules:
  0.0 437.7 jit_solution(1554293441669828181)
XLA Ops:
  0.7 7.6 %all_gather.28 = bf16[1,64,2048]{2,1,0:T(8,128)(2,1)S(1)} all-gather(bf16[1,64,512]{2,1,0:T(8,128)(2,1)} %param.20), channel_id=1, replica_groups=mesh['day'=8,'pt'=4] {'pt'}, dimensions={2}, use_global_device_ids=true | all-gather | bytes 327680 | tf_op jit(solution)/shard_map/all_gather | solution.py:47
  14.2 7.4 %all_gather.29 = f32[1,64,2048]{2,1,0:T(8,128)S(1)} all-gather(f32[1,64,512]{2,1,0:T(8,128)} %param.22), channel_id=1, replica_groups=mesh['day'=8,'pt'=4] {'pt'}, dimensions={2}, use_global_device_ids=true | all-gather | bytes 655360 | tf_op jit(solution)/shard_map/all_gather | solution.py:48
  30.0 338.5 %while.72 = (s32[]{:T(128)}, bf16[16,2048]{1,0:T(8,128)(2,1)S(1)}, bf16[16,2048]{1,0:T(8,128)(2,1)S(1)}, f32[64,512]{1,0:T(8,128)S(1)}, f32[64,512]{1,0:T(8,128)...) while((s32[]{:T(128)}, bf16[16,2048]{1,0:T(8,128)(2,1)S(1)}, ...), condition=%wide.region_14.15_spmd.clone.clone, body=%wide.region_3.14_spmd.clone.clone.sunk | while | flops 87085088 | bytes 2573997 | solution.py:157
  32.0 5.4 %all_gather.38 = f32[16,2048]{1,0:T(8,128)S(1)} all-gather(f32[16,512]{1,0:T(8,128)S(1)} %get-tuple-element.1308), channel_id=1, replica_groups=mesh['day'=8,'pt'=4] {'pt'}, dimensions={1}, use_global_device_ids=true | all-gather | bytes 163840 | tf_op jit(solution)/shard_map/while/body/eval_jaxpr/all_gather | solution.py:125
  56.2 5.4 %all_gather.38 = f32[16,2048]{1,0:T(8,128)S(1)} all-gather(f32[16,512]{1,0:T(8,128)S(1)} %get-tuple-element.1308), channel_id=1, replica_groups=mesh['day'=8,'pt'=4] {'pt'}, dimensions={1}, use_global_device_ids=true | all-gather | bytes 163840 | tf_op jit(solution)/shard_map/while/body/eval_jaxpr/all_gather | solution.py:125
  68.0 9.9 %collective-permute-start = (bf16[16,2048]{1,0:T(8,128)(2,1)S(1)}, bf16[16,2048]{1,0:T(8,128)(2,1)S(1)}, u32[]{:S(2)}, u32[]{:S(2)}) collective-permute-start(bf16[16,2048]{1,0:T(8,128)(2,1)S(1)} %get-tuple-element.1314), channel_id=1, source_target_pairs={{0,4},{4,8},{8,12},{12,16},{16,20},{20,24},{24,28},{1,5},{5,9},{9,... | collective-permute-start | bytes 196616 | tf_op jit(solution)/shard_map/while/body/eval_jaxpr/ppermute | solution.py:27
  86.0 5.4 %all_gather.38 = f32[16,2048]{1,0:T(8,128)S(1)} all-gather(f32[16,512]{1,0:T(8,128)S(1)} %get-tuple-element.1308), channel_id=1, replica_groups=mesh['day'=8,'pt'=4] {'pt'}, dimensions={1}, use_global_device_ids=true | all-gather | bytes 163840 | tf_op jit(solution)/shard_map/while/body/eval_jaxpr/all_gather | solution.py:125
  97.8 9.3 %collective-permute-start = (bf16[16,2048]{1,0:T(8,128)(2,1)S(1)}, bf16[16,2048]{1,0:T(8,128)(2,1)S(1)}, u32[]{:S(2)}, u32[]{:S(2)}) collective-permute-start(bf16[16,2048]{1,0:T(8,128)(2,1)S(1)} %get-tuple-element.1314), channel_id=1, source_target_pairs={{0,4},{4,8},{8,12},{12,16},{16,20},{20,24},{24,28},{1,5},{5,9},{9,... | collective-permute-start | bytes 196616 | tf_op jit(solution)/shard_map/while/body/eval_jaxpr/ppermute | solution.py:27
  115.3 5.4 %all_gather.38 = f32[16,2048]{1,0:T(8,128)S(1)} all-gather(f32[16,512]{1,0:T(8,128)S(1)} %get-tuple-element.1308), channel_id=1, replica_groups=mesh['day'=8,'pt'=4] {'pt'}, dimensions={1}, use_global_device_ids=true | all-gather | bytes 163840 | tf_op jit(solution)/shard_map/while/body/eval_jaxpr/all_gather | solution.py:125
  127.0 9.3 %collective-permute-start = (bf16[16,2048]{1,0:T(8,128)(2,1)S(1)}, bf16[16,2048]{1,0:T(8,128)(2,1)S(1)}, u32[]{:S(2)}, u32[]{:S(2)}) collective-permute-start(bf16[16,2048]{1,0:T(8,128)(2,1)S(1)} %get-tuple-element.1314), channel_id=1, source_target_pairs={{0,4},{4,8},{8,12},{12,16},{16,20},{20,24},{24,28},{1,5},{5,9},{9,... | collective-permute-start | bytes 196616 | tf_op jit(solution)/shard_map/while/body/eval_jaxpr/ppermute | solution.py:27
  144.5 5.4 %all_gather.38 = f32[16,2048]{1,0:T(8,128)S(1)} all-gather(f32[16,512]{1,0:T(8,128)S(1)} %get-tuple-element.1308), channel_id=1, replica_groups=mesh['day'=8,'pt'=4] {'pt'}, dimensions={1}, use_global_device_ids=true | all-gather | bytes 163840 | tf_op jit(solution)/shard_map/while/body/eval_jaxpr/all_gather | solution.py:125
  156.3 9.3 %collective-permute-start = (bf16[16,2048]{1,0:T(8,128)(2,1)S(1)}, bf16[16,2048]{1,0:T(8,128)(2,1)S(1)}, u32[]{:S(2)}, u32[]{:S(2)}) collective-permute-start(bf16[16,2048]{1,0:T(8,128)(2,1)S(1)} %get-tuple-element.1314), channel_id=1, source_target_pairs={{0,4},{4,8},{8,12},{12,16},{16,20},{20,24},{24,28},{1,5},{5,9},{9,... | collective-permute-start | bytes 196616 | tf_op jit(solution)/shard_map/while/body/eval_jaxpr/ppermute | solution.py:27
  173.8 5.4 %all_gather.38 = f32[16,2048]{1,0:T(8,128)S(1)} all-gather(f32[16,512]{1,0:T(8,128)S(1)} %get-tuple-element.1308), channel_id=1, replica_groups=mesh['day'=8,'pt'=4] {'pt'}, dimensions={1}, use_global_device_ids=true | all-gather | bytes 163840 | tf_op jit(solution)/shard_map/while/body/eval_jaxpr/all_gather | solution.py:125
  185.5 11.0 %collective-permute-start = (bf16[16,2048]{1,0:T(8,128)(2,1)S(1)}, bf16[16,2048]{1,0:T(8,128)(2,1)S(1)}, u32[]{:S(2)}, u32[]{:S(2)}) collective-permute-start(bf16[16,2048]{1,0:T(8,128)(2,1)S(1)} %get-tuple-element.1314), channel_id=1, source_target_pairs={{0,4},{4,8},{8,12},{12,16},{16,20},{20,24},{24,28},{1,5},{5,9},{9,... | collective-permute-start | bytes 196616 | tf_op jit(solution)/shard_map/while/body/eval_jaxpr/ppermute | solution.py:27
  198.4 17.1 %collective-permute-done.1 = bf16[16,2048]{1,0:T(8,128)(2,1)S(1)} collective-permute-done((bf16[16,2048]{1,0:T(8,128)(2,1)S(1)}, bf16[16,2048]{1,0:T(8,128)(2,1)S(1)}, u32[]{:S(2)}, u32[]{:S(2)}) %collective-permute-start.1) | collective-permute-done | bytes 65568 | tf_op jit(solution)/shard_map/while/body/eval_jaxpr/ppermute | solution.py:27
  217.6 5.4 %all_gather.38 = f32[16,2048]{1,0:T(8,128)S(1)} all-gather(f32[16,512]{1,0:T(8,128)S(1)} %get-tuple-element.1308), channel_id=1, replica_groups=mesh['day'=8,'pt'=4] {'pt'}, dimensions={1}, use_global_device_ids=true | all-gather | bytes 163840 | tf_op jit(solution)/shard_map/while/body/eval_jaxpr/all_gather | solution.py:125
  229.3 11.2 %collective-permute-start = (bf16[16,2048]{1,0:T(8,128)(2,1)S(1)}, bf16[16,2048]{1,0:T(8,128)(2,1)S(1)}, u32[]{:S(2)}, u32[]{:S(2)}) collective-permute-start(bf16[16,2048]{1,0:T(8,128)(2,1)S(1)} %get-tuple-element.1314), channel_id=1, source_target_pairs={{0,4},{4,8},{8,12},{12,16},{16,20},{20,24},{24,28},{1,5},{5,9},{9,... | collective-permute-start | bytes 196616 | tf_op jit(solution)/shard_map/while/body/eval_jaxpr/ppermute | solution.py:27
  246.6 7.0 %conditional.8 = (f32[16,512]{1,0:T(8,128)}) conditional(s32[]{:T(128)} %convert_element_type.133, () %tuple.157, (bf16[16,2048]{1,0:T(8,128)(2,1)S(1)}, f32[2048]{0:T(1024)S(1)}, f32[512]{0:T(512)S(1)}, bf16[64,2048]{1,0:T(8,128)(2,1)S(1)}, bf16[64,512]{1,0:T(8,128)(2,1)S(1)}) %tuple.158), branch_computations={%region_9.9_spmd, %region_10.12_spmd} | conditional | flops 43270152 | bytes 222992 | solution.py:117
  246.6 7.0 %while.69 = (s32[]{:T(128)}, f32[16,512]{1,0:T(8,128)}, bf16[16,2048]{1,0:T(8,128)(2,1)S(1)}, f32[2048]{0:T(1024)S(1)}, f32[512]{0:T(512)S(1)}, /*index=5*/bf16[...) while((s32[]{:T(128)}, f32[16,512]{1,0:T(8,128)}, ...), condition=%wide.region_12.11_spmd.clone, body=%wide.region_11.10_spmd.clone.sunk | while | flops 43270152 | bytes 222888 | solution.py:86
  255.1 5.4 %all_gather.38 = f32[16,2048]{1,0:T(8,128)S(1)} all-gather(f32[16,512]{1,0:T(8,128)S(1)} %get-tuple-element.1308), channel_id=1, replica_groups=mesh['day'=8,'pt'=4] {'pt'}, dimensions={1}, use_global_device_ids=true | all-gather | bytes 163840 | tf_op jit(solution)/shard_map/while/body/eval_jaxpr/all_gather | solution.py:125
  266.8 7.5 %collective-permute-start = (bf16[16,2048]{1,0:T(8,128)(2,1)S(1)}, bf16[16,2048]{1,0:T(8,128)(2,1)S(1)}, u32[]{:S(2)}, u32[]{:S(2)}) collective-permute-start(bf16[16,2048]{1,0:T(8,128)(2,1)S(1)} %get-tuple-element.1314), channel_id=1, source_target_pairs={{0,4},{4,8},{8,12},{12,16},{16,20},{20,24},{24,28},{1,5},{5,9},{9,... | collective-permute-start | bytes 196616 | tf_op jit(solution)/shard_map/while/body/eval_jaxpr/ppermute | solution.py:27
  280.5 7.0 %conditional.8 = (f32[16,512]{1,0:T(8,128)}) conditional(s32[]{:T(128)} %convert_element_type.133, () %tuple.157, (bf16[16,2048]{1,0:T(8,128)(2,1)S(1)}, f32[2048]{0:T(1024)S(1)}, f32[512]{0:T(512)S(1)}, bf16[64,2048]{1,0:T(8,128)(2,1)S(1)}, bf16[64,512]{1,0:T(8,128)(2,1)S(1)}) %tuple.158), branch_computations={%region_9.9_spmd, %region_10.12_spmd} | conditional | flops 43270152 | bytes 222992 | solution.py:117
  280.5 7.0 %while.69 = (s32[]{:T(128)}, f32[16,512]{1,0:T(8,128)}, bf16[16,2048]{1,0:T(8,128)(2,1)S(1)}, f32[2048]{0:T(1024)S(1)}, f32[512]{0:T(512)S(1)}, /*index=5*/bf16[...) while((s32[]{:T(128)}, f32[16,512]{1,0:T(8,128)}, ...), condition=%wide.region_12.11_spmd.clone, body=%wide.region_11.10_spmd.clone.sunk | while | flops 43270152 | bytes 222888 | solution.py:86
  288.9 5.4 %all_gather.38 = f32[16,2048]{1,0:T(8,128)S(1)} all-gather(f32[16,512]{1,0:T(8,128)S(1)} %get-tuple-element.1308), channel_id=1, replica_groups=mesh['day'=8,'pt'=4] {'pt'}, dimensions={1}, use_global_device_ids=true | all-gather | bytes 163840 | tf_op jit(solution)/shard_map/while/body/eval_jaxpr/all_gather | solution.py:125
  311.6 7.0 %conditional.8 = (f32[16,512]{1,0:T(8,128)}) conditional(s32[]{:T(128)} %convert_element_type.133, () %tuple.157, (bf16[16,2048]{1,0:T(8,128)(2,1)S(1)}, f32[2048]{0:T(1024)S(1)}, f32[512]{0:T(512)S(1)}, bf16[64,2048]{1,0:T(8,128)(2,1)S(1)}, bf16[64,512]{1,0:T(8,128)(2,1)S(1)}) %tuple.158), branch_computations={%region_9.9_spmd, %region_10.12_spmd} | conditional | flops 43270152 | bytes 222992 | solution.py:117
  311.6 7.0 %while.69 = (s32[]{:T(128)}, f32[16,512]{1,0:T(8,128)}, bf16[16,2048]{1,0:T(8,128)(2,1)S(1)}, f32[2048]{0:T(1024)S(1)}, f32[512]{0:T(512)S(1)}, /*index=5*/bf16[...) while((s32[]{:T(128)}, f32[16,512]{1,0:T(8,128)}, ...), condition=%wide.region_12.11_spmd.clone, body=%wide.region_11.10_spmd.clone.sunk | while | flops 43270152 | bytes 222888 | solution.py:86
  320.0 5.4 %all_gather.38 = f32[16,2048]{1,0:T(8,128)S(1)} all-gather(f32[16,512]{1,0:T(8,128)S(1)} %get-tuple-element.1308), channel_id=1, replica_groups=mesh['day'=8,'pt'=4] {'pt'}, dimensions={1}, use_global_device_ids=true | all-gather | bytes 163840 | tf_op jit(solution)/shard_map/while/body/eval_jaxpr/all_gather | solution.py:125
  340.8 7.0 %conditional.8 = (f32[16,512]{1,0:T(8,128)}) conditional(s32[]{:T(128)} %convert_element_type.133, () %tuple.157, (bf16[16,2048]{1,0:T(8,128)(2,1)S(1)}, f32[2048]{0:T(1024)S(1)}, f32[512]{0:T(512)S(1)}, bf16[64,2048]{1,0:T(8,128)(2,1)S(1)}, bf16[64,512]{1,0:T(8,128)(2,1)S(1)}) %tuple.158), branch_computations={%region_9.9_spmd, %region_10.12_spmd} | conditional | flops 43270152 | bytes 222992 | solution.py:117
  340.8 7.0 %while.69 = (s32[]{:T(128)}, f32[16,512]{1,0:T(8,128)}, bf16[16,2048]{1,0:T(8,128)(2,1)S(1)}, f32[2048]{0:T(1024)S(1)}, f32[512]{0:T(512)S(1)}, /*index=5*/bf16[...) while((s32[]{:T(128)}, f32[16,512]{1,0:T(8,128)}, ...), condition=%wide.region_12.11_spmd.clone, body=%wide.region_11.10_spmd.clone.sunk | while | flops 43270152 | bytes 222888 | solution.py:86
  373.8 25.9 %while.70 = (s32[]{:T(128)}, f32[8,2048]{1,0:T(8,128)S(1)}, s32[8]{0:T(128)S(1)}, f32[2048]{0:T(1024)S(1)}, f32[2048]{0:T(1024)S(1)}, /*index=5*/f32[2048]{0:T(1...) while((s32[]{:T(128)}, f32[8,2048]{1,0:T(8,128)S(1)}, ...), condition=%wide.region_20.21_spmd, body=%wide.region_19.20_spmd.sunk | while | flops 75497480 | bytes 4528319 | solution.py:185
  401.0 29.2 %while.71 = (s32[]{:T(128)}, f32[8,256]{1,0:T(8,128)S(1)}, s32[8]{0:T(128)S(1)}, f32[2048]{0:T(1024)S(1)}, f32[2048]{0:T(1024)S(1)}, /*index=5*/bf16[64,2048]{1,...) while((s32[]{:T(128)}, f32[8,256]{1,0:T(8,128)S(1)}, ...), condition=%wide.region_23.24_spmd, body=%wide.region_22.23_spmd.sunk | while | flops 75497480 | bytes 4511931 | solution.py:194
  430.2 6.8 %all-reduce = f32[2048]{0:T(1024)S(1)} all-reduce(f32[2048]{0:T(1024)S(1)} %bitcast.86), channel_id=2, replica_groups=mesh['day'=8,'pt'=4] {'pt'}, use_global_device_ids=true, to_apply=%region_24.25.clone | all-reduce | flops 2048 | bytes 16384
  (317 shorter events, 273.7 us)
Async XLA Ops:
  0.6 27.7 %copy-start.6 = (u32[32]{0:T(128)S(1)}, u32[32]{0:T(128)}, u32[]{:S(2)}) copy-start(u32[32]{0:T(128)} %constant.212) | copy-start | bytes 388
  0.6 26.3 %copy-start.3 = (bf16[1,64,512]{2,1,0:T(8,128)(2,1)S(1)}, bf16[1,64,512]{2,1,0:T(8,128)(2,1)}, u32[]{:S(2)}) copy-start(bf16[1,64,512]{2,1,0:T(8,128)(2,1)} %param.20) | copy-start | bytes 196612
  0.7 29.0 %copy-start.4 = (bf16[1,64,2048]{2,1,0:T(8,128)(2,1)S(1)}, bf16[1,64,2048]{2,1,0:T(8,128)(2,1)}, u32[]{:S(2)}) copy-start(bf16[1,64,2048]{2,1,0:T(8,128)(2,1)} %param.21) | copy-start | bytes 786436
  8.3 21.4 %collective-permute-start.3 = (bf16[1,64,2048]{2,1,0:T(8,128)(2,1)S(1)}, bf16[1,64,2048]{2,1,0:T(8,128)(2,1)S(1)}, u32[]{:S(2)}, u32[]{:S(2)}) collective-permute-start(bf16[1,64,2048]{2,1,0:T(8,128)(2,1)S(1)} %all_gather.28), channel_id=1, source_target_pairs={{4,0},{8,4},{12,8},{16,12},{20,16},{24,20},{28,24},{5,1},{9,5},{13... | collective-permute-start | bytes 786440 | tf_op jit(solution)/shard_map/ppermute | solution.py:17
  9.5 20.2 %collective-permute-start.2 = (bf16[1,64,2048]{2,1,0:T(8,128)(2,1)S(1)}, bf16[1,64,2048]{2,1,0:T(8,128)(2,1)S(1)}, u32[]{:S(2)}, u32[]{:S(2)}) collective-permute-start(bf16[1,64,2048]{2,1,0:T(8,128)(2,1)S(1)} %all_gather.28), channel_id=1, source_target_pairs={{0,4},{4,8},{8,12},{12,16},{16,20},{20,24},{24,28},{1,5},{5,9},{9,... | collective-permute-start | bytes 786440 | tf_op jit(solution)/shard_map/ppermute | solution.py:15
  29.9 338.6 %copy-start.2 = (f32[1,64,512]{2,1,0:T(8,128)S(1)}, f32[1,64,512]{2,1,0:T(8,128)}, u32[]{:S(2)}) copy-start(f32[1,64,512]{2,1,0:T(8,128)} %param.22) | copy-start | bytes 393220
  30.0 338.6 %copy-start.5 = (f32[1,512]{1,0:T(1,128)S(1)}, f32[1,512]{1,0:T(1,128)}, u32[]{:S(2)}) copy-start(f32[1,512]{1,0:T(1,128)} %param.23) | copy-start | bytes 6148
  43.8 6.2 %collective-permute-start = (bf16[16,2048]{1,0:T(8,128)(2,1)S(1)}, bf16[16,2048]{1,0:T(8,128)(2,1)S(1)}, u32[]{:S(2)}, u32[]{:S(2)}) collective-permute-start(bf16[16,2048]{1,0:T(8,128)(2,1)S(1)} %get-tuple-element.1314), channel_id=1, source_target_pairs={{0,4},{4,8},{8,12},{12,16},{16,20},{20,24},{24,28},{1,5},{5,9},{9,... | collective-permute-start | bytes 196616 | tf_op jit(solution)/shard_map/while/body/eval_jaxpr/ppermute | solution.py:27
  48.1 6.2 %collective-permute-start.1 = (bf16[16,2048]{1,0:T(8,128)(2,1)S(1)}, bf16[16,2048]{1,0:T(8,128)(2,1)S(1)}, u32[]{:S(2)}, u32[]{:S(2)}) collective-permute-start(bf16[16,2048]{1,0:T(8,128)(2,1)S(1)} %get-tuple-element.1315), channel_id=1, source_target_pairs={{4,0},{8,4},{12,8},{16,12},{20,16},{24,20},{28,24},{5,1},{9,5},{13... | collective-permute-start | bytes 196616 | tf_op jit(solution)/shard_map/while/body/eval_jaxpr/ppermute | solution.py:27
  68.0 11.8 %collective-permute-start = (bf16[16,2048]{1,0:T(8,128)(2,1)S(1)}, bf16[16,2048]{1,0:T(8,128)(2,1)S(1)}, u32[]{:S(2)}, u32[]{:S(2)}) collective-permute-start(bf16[16,2048]{1,0:T(8,128)(2,1)S(1)} %get-tuple-element.1314), channel_id=1, source_target_pairs={{0,4},{4,8},{8,12},{12,16},{16,20},{20,24},{24,28},{1,5},{5,9},{9,... | collective-permute-start | bytes 196616 | tf_op jit(solution)/shard_map/while/body/eval_jaxpr/ppermute | solution.py:27
  77.9 6.2 %collective-permute-start.1 = (bf16[16,2048]{1,0:T(8,128)(2,1)S(1)}, bf16[16,2048]{1,0:T(8,128)(2,1)S(1)}, u32[]{:S(2)}, u32[]{:S(2)}) collective-permute-start(bf16[16,2048]{1,0:T(8,128)(2,1)S(1)} %get-tuple-element.1315), channel_id=1, source_target_pairs={{4,0},{8,4},{12,8},{16,12},{20,16},{24,20},{28,24},{5,1},{9,5},{13... | collective-permute-start | bytes 196616 | tf_op jit(solution)/shard_map/while/body/eval_jaxpr/ppermute | solution.py:27
  97.8 11.2 %collective-permute-start = (bf16[16,2048]{1,0:T(8,128)(2,1)S(1)}, bf16[16,2048]{1,0:T(8,128)(2,1)S(1)}, u32[]{:S(2)}, u32[]{:S(2)}) collective-permute-start(bf16[16,2048]{1,0:T(8,128)(2,1)S(1)} %get-tuple-element.1314), channel_id=1, source_target_pairs={{0,4},{4,8},{8,12},{12,16},{16,20},{20,24},{24,28},{1,5},{5,9},{9,... | collective-permute-start | bytes 196616 | tf_op jit(solution)/shard_map/while/body/eval_jaxpr/ppermute | solution.py:27
  107.1 6.2 %collective-permute-start.1 = (bf16[16,2048]{1,0:T(8,128)(2,1)S(1)}, bf16[16,2048]{1,0:T(8,128)(2,1)S(1)}, u32[]{:S(2)}, u32[]{:S(2)}) collective-permute-start(bf16[16,2048]{1,0:T(8,128)(2,1)S(1)} %get-tuple-element.1315), channel_id=1, source_target_pairs={{4,0},{8,4},{12,8},{16,12},{20,16},{24,20},{28,24},{5,1},{9,5},{13... | collective-permute-start | bytes 196616 | tf_op jit(solution)/shard_map/while/body/eval_jaxpr/ppermute | solution.py:27
  127.0 11.2 %collective-permute-start = (bf16[16,2048]{1,0:T(8,128)(2,1)S(1)}, bf16[16,2048]{1,0:T(8,128)(2,1)S(1)}, u32[]{:S(2)}, u32[]{:S(2)}) collective-permute-start(bf16[16,2048]{1,0:T(8,128)(2,1)S(1)} %get-tuple-element.1314), channel_id=1, source_target_pairs={{0,4},{4,8},{8,12},{12,16},{16,20},{20,24},{24,28},{1,5},{5,9},{9,... | collective-permute-start | bytes 196616 | tf_op jit(solution)/shard_map/while/body/eval_jaxpr/ppermute | solution.py:27
  136.4 6.2 %collective-permute-start.1 = (bf16[16,2048]{1,0:T(8,128)(2,1)S(1)}, bf16[16,2048]{1,0:T(8,128)(2,1)S(1)}, u32[]{:S(2)}, u32[]{:S(2)}) collective-permute-start(bf16[16,2048]{1,0:T(8,128)(2,1)S(1)} %get-tuple-element.1315), channel_id=1, source_target_pairs={{4,0},{8,4},{12,8},{16,12},{20,16},{24,20},{28,24},{5,1},{9,5},{13... | collective-permute-start | bytes 196616 | tf_op jit(solution)/shard_map/while/body/eval_jaxpr/ppermute | solution.py:27
  156.3 11.2 %collective-permute-start = (bf16[16,2048]{1,0:T(8,128)(2,1)S(1)}, bf16[16,2048]{1,0:T(8,128)(2,1)S(1)}, u32[]{:S(2)}, u32[]{:S(2)}) collective-permute-start(bf16[16,2048]{1,0:T(8,128)(2,1)S(1)} %get-tuple-element.1314), channel_id=1, source_target_pairs={{0,4},{4,8},{8,12},{12,16},{16,20},{20,24},{24,28},{1,5},{5,9},{9,... | collective-permute-start | bytes 196616 | tf_op jit(solution)/shard_map/while/body/eval_jaxpr/ppermute | solution.py:27
  165.6 6.2 %collective-permute-start.1 = (bf16[16,2048]{1,0:T(8,128)(2,1)S(1)}, bf16[16,2048]{1,0:T(8,128)(2,1)S(1)}, u32[]{:S(2)}, u32[]{:S(2)}) collective-permute-start(bf16[16,2048]{1,0:T(8,128)(2,1)S(1)} %get-tuple-element.1315), channel_id=1, source_target_pairs={{4,0},{8,4},{12,8},{16,12},{20,16},{24,20},{28,24},{5,1},{9,5},{13... | collective-permute-start | bytes 196616 | tf_op jit(solution)/shard_map/while/body/eval_jaxpr/ppermute | solution.py:27
  185.5 12.9 %collective-permute-start = (bf16[16,2048]{1,0:T(8,128)(2,1)S(1)}, bf16[16,2048]{1,0:T(8,128)(2,1)S(1)}, u32[]{:S(2)}, u32[]{:S(2)}) collective-permute-start(bf16[16,2048]{1,0:T(8,128)(2,1)S(1)} %get-tuple-element.1314), channel_id=1, source_target_pairs={{0,4},{4,8},{8,12},{12,16},{16,20},{20,24},{24,28},{1,5},{5,9},{9,... | collective-permute-start | bytes 196616 | tf_op jit(solution)/shard_map/while/body/eval_jaxpr/ppermute | solution.py:27
  196.5 19.0 %collective-permute-start.1 = (bf16[16,2048]{1,0:T(8,128)(2,1)S(1)}, bf16[16,2048]{1,0:T(8,128)(2,1)S(1)}, u32[]{:S(2)}, u32[]{:S(2)}) collective-permute-start(bf16[16,2048]{1,0:T(8,128)(2,1)S(1)} %get-tuple-element.1315), channel_id=1, source_target_pairs={{4,0},{8,4},{12,8},{16,12},{20,16},{24,20},{28,24},{5,1},{9,5},{13... | collective-permute-start | bytes 196616 | tf_op jit(solution)/shard_map/while/body/eval_jaxpr/ppermute | solution.py:27
  229.3 13.1 %collective-permute-start = (bf16[16,2048]{1,0:T(8,128)(2,1)S(1)}, bf16[16,2048]{1,0:T(8,128)(2,1)S(1)}, u32[]{:S(2)}, u32[]{:S(2)}) collective-permute-start(bf16[16,2048]{1,0:T(8,128)(2,1)S(1)} %get-tuple-element.1314), channel_id=1, source_target_pairs={{0,4},{4,8},{8,12},{12,16},{16,20},{20,24},{24,28},{1,5},{5,9},{9,... | collective-permute-start | bytes 196616 | tf_op jit(solution)/shard_map/while/body/eval_jaxpr/ppermute | solution.py:27
  240.5 6.2 %collective-permute-start.1 = (bf16[16,2048]{1,0:T(8,128)(2,1)S(1)}, bf16[16,2048]{1,0:T(8,128)(2,1)S(1)}, u32[]{:S(2)}, u32[]{:S(2)}) collective-permute-start(bf16[16,2048]{1,0:T(8,128)(2,1)S(1)} %get-tuple-element.1315), channel_id=1, source_target_pairs={{4,0},{8,4},{12,8},{16,12},{20,16},{24,20},{28,24},{5,1},{9,5},{13... | collective-permute-start | bytes 196616 | tf_op jit(solution)/shard_map/while/body/eval_jaxpr/ppermute | solution.py:27
  266.8 9.4 %collective-permute-start = (bf16[16,2048]{1,0:T(8,128)(2,1)S(1)}, bf16[16,2048]{1,0:T(8,128)(2,1)S(1)}, u32[]{:S(2)}, u32[]{:S(2)}) collective-permute-start(bf16[16,2048]{1,0:T(8,128)(2,1)S(1)} %get-tuple-element.1314), channel_id=1, source_target_pairs={{0,4},{4,8},{8,12},{12,16},{16,20},{20,24},{24,28},{1,5},{5,9},{9,... | collective-permute-start | bytes 196616 | tf_op jit(solution)/shard_map/while/body/eval_jaxpr/ppermute | solution.py:27
  274.3 6.2 %collective-permute-start.1 = (bf16[16,2048]{1,0:T(8,128)(2,1)S(1)}, bf16[16,2048]{1,0:T(8,128)(2,1)S(1)}, u32[]{:S(2)}, u32[]{:S(2)}) collective-permute-start(bf16[16,2048]{1,0:T(8,128)(2,1)S(1)} %get-tuple-element.1315), channel_id=1, source_target_pairs={{4,0},{8,4},{12,8},{16,12},{20,16},{24,20},{28,24},{5,1},{9,5},{13... | collective-permute-start | bytes 196616 | tf_op jit(solution)/shard_map/while/body/eval_jaxpr/ppermute | solution.py:27
  300.6 6.6 %collective-permute-start = (bf16[16,2048]{1,0:T(8,128)(2,1)S(1)}, bf16[16,2048]{1,0:T(8,128)(2,1)S(1)}, u32[]{:S(2)}, u32[]{:S(2)}) collective-permute-start(bf16[16,2048]{1,0:T(8,128)(2,1)S(1)} %get-tuple-element.1314), channel_id=1, source_target_pairs={{0,4},{4,8},{8,12},{12,16},{16,20},{20,24},{24,28},{1,5},{5,9},{9,... | collective-permute-start | bytes 196616 | tf_op jit(solution)/shard_map/while/body/eval_jaxpr/ppermute | solution.py:27
  305.4 6.2 %collective-permute-start.1 = (bf16[16,2048]{1,0:T(8,128)(2,1)S(1)}, bf16[16,2048]{1,0:T(8,128)(2,1)S(1)}, u32[]{:S(2)}, u32[]{:S(2)}) collective-permute-start(bf16[16,2048]{1,0:T(8,128)(2,1)S(1)} %get-tuple-element.1315), channel_id=1, source_target_pairs={{4,0},{8,4},{12,8},{16,12},{20,16},{24,20},{28,24},{5,1},{9,5},{13... | collective-permute-start | bytes 196616 | tf_op jit(solution)/shard_map/while/body/eval_jaxpr/ppermute | solution.py:27
  331.7 4.8 %collective-permute-start = (bf16[16,2048]{1,0:T(8,128)(2,1)S(1)}, bf16[16,2048]{1,0:T(8,128)(2,1)S(1)}, u32[]{:S(2)}, u32[]{:S(2)}) collective-permute-start(bf16[16,2048]{1,0:T(8,128)(2,1)S(1)} %get-tuple-element.1314), channel_id=1, source_target_pairs={{0,4},{4,8},{8,12},{12,16},{16,20},{20,24},{24,28},{1,5},{5,9},{9,... | collective-permute-start | bytes 196616 | tf_op jit(solution)/shard_map/while/body/eval_jaxpr/ppermute | solution.py:27
  334.6 6.2 %collective-permute-start.1 = (bf16[16,2048]{1,0:T(8,128)(2,1)S(1)}, bf16[16,2048]{1,0:T(8,128)(2,1)S(1)}, u32[]{:S(2)}, u32[]{:S(2)}) collective-permute-start(bf16[16,2048]{1,0:T(8,128)(2,1)S(1)} %get-tuple-element.1315), channel_id=1, source_target_pairs={{4,0},{8,4},{12,8},{16,12},{20,16},{24,20},{28,24},{5,1},{9,5},{13... | collective-permute-start | bytes 196616 | tf_op jit(solution)/shard_map/while/body/eval_jaxpr/ppermute | solution.py:27
  361.0 3.4 collective-permute-start
  362.3 6.2 %collective-permute-start.1 = (bf16[16,2048]{1,0:T(8,128)(2,1)S(1)}, bf16[16,2048]{1,0:T(8,128)(2,1)S(1)}, u32[]{:S(2)}, u32[]{:S(2)}) collective-permute-start(bf16[16,2048]{1,0:T(8,128)(2,1)S(1)} %get-tuple-element.1315), channel_id=1, source_target_pairs={{4,0},{8,4},{12,8},{16,12},{20,16},{24,20},{28,24},{5,1},{9,5},{13... | collective-permute-start | bytes 196616 | tf_op jit(solution)/shard_map/while/body/eval_jaxpr/ppermute | solution.py:27
  368.5 5.3 %copy-start = (f32[64,512]{1,0:T(8,128)}, f32[64,512]{1,0:T(8,128)S(1)}, u32[]{:S(2)}) copy-start(f32[64,512]{1,0:T(8,128)S(1)} %get-tuple-element.741) | copy-start | bytes 393220
  368.5 5.3 %copy-start.1 = (f32[64,512]{1,0:T(8,128)}, f32[64,512]{1,0:T(8,128)S(1)}, u32[]{:S(2)}) copy-start(f32[64,512]{1,0:T(8,128)S(1)} %get-tuple-element.742) | copy-start | bytes 393220
where the time goes:
time: 441 us; the launch traced here: 438 us
  blocking collectives  151 us (34%)
  starting transfers between devices  101 us (23%)
  waiting for transfers between devices  65.4 us (15%)
  matrix products  58.2 us (13%)
  local copies, waits for them, and re-layouts  25.9 us (6%)
  other arithmetic  21.6 us (5%)
  loops' own time  11.7 us (3%)
    ppermute x22, starting transfers between devices, shifted(): return lax.ppermute(block, axis, route)  95 us
    ppermute x22, waiting for transfers between devices, shifted(): return lax.ppermute(block, axis, route)  65.4 us
    all_gather x11, blocking collectives, one_step(): lax.all_gather(backward_piece, 'pt', axis=1, tiled=True)  59.5 us
    all_gather x11, blocking collectives, one_step(): lax.all_gather(forward_piece, 'pt', axis=1, tiled=True)  59.4 us
    dot_general x16, matrix products, add_rows(): jnp.dot(sent_part, kernel_rows(source_pts, source_norm, block_index), pre...  27 us
    dot_general x8, matrix products, ratio_part(): jnp.dot(fit_rows(block_index), inverse, precision=lax.Precision.HIGHEST)  13.8 us
    another operation x18, local copies, waits for them, and re-layouts  11.1 us
    dynamic_slice x16, local copies, waits for them, and re-layouts, shards(): lax.map(density_part, jnp.arange(fit_blocks))  9.38 us
  transfers between devices with their start and end apart: 24, of which 22 were waited for; matrix products, arithmetic and copies ran while one was open for 0% of the time, Pallas kernels for 0%

commit v1 on v0

--- a/solution.py
+++ b/solution.py
@@ -2,6 +2,22 @@
 import jax.numpy as jnp
 from jax import lax
 from jax.sharding import PartitionSpec as P
+
+
+def take_series_all(buf):
+    dev_count = lax.axis_size("pt")
+    panels = [(u, (u + 1) % dev_count) for u in range(dev_count)]
+    seen = [(u, (u - 1) % dev_count) for u in range(dev_count)]
+    finding, odd = ([buf], [buf])
+    for _ in range(dev_count // 2):
+        finding.append(lax.ppermute(finding[-1], "pt", panels))
+    for _ in range((dev_count - 1) // 2):
+        odd.append(lax.ppermute(odd[-1], "pt", seen))
+    return jnp.roll(
+        jnp.concatenate([*finding[::-1], *odd[1:]], axis=1),
+        (lax.axis_index("pt") - dev_count // 2) * buf.shape[1],
+        axis=1,
+    )
 
 
 def with_halo(cells, sides, width):
@@ -122,7 +138,7 @@
         backward_piece = jnp.where(day_index == day_count - 1, seed_rows, backward_got)
         forward_full, backward_full = (
             lax.all_gather(forward_piece, "pt", axis=1, tiled=True),
-            lax.all_gather(backward_piece, "pt", axis=1, tiled=True),
+            take_series_all(backward_piece),
         )
         forward_own, forward_all = settle(forward_piece, forward_full, forward_ok)
         backward_own, backward_all = settle(backward_piece, backward_full, backward_ok)

time: 441 us -> 415 us (0.941)
  blocking collectives: 151 us -> 94.1 us
  starting transfers between devices: 101 us -> 121 us
  waiting for transfers between devices: 65.4 us -> 75.2 us
    all_gather x11 -> x0, blocking collectives: 59.5 us -> none  [one_step(): lax.all_gather(backward_piece, 'pt', axis=1, tiled=True)]
    ppermute x0 -> x33, starting transfers between devices: none -> 19.7 us  [the longest x11 18.7 us: take_series_all(): odd.append(lax.ppermute(odd[-1], 'pt', seen))]
    ppermute x0 -> x33, waiting for transfers between devices: none -> 9.84 us  [the longest x22 9.81 us: take_series_all(): finding.append(lax.ppermute(finding[-1], 'pt', panels))]
  transfers between devices with their start and end apart: 24 -> 57, of which waited for: 22 -> 33; matrix products, arithmetic and copies ran while one was open for 0% -> 2% of each run, Pallas kernels for 0% -> 0%
where the time goes in v1:
time: 415 us; the launch traced here: 412 us
  starting transfers between devices  121 us (29%)
  blocking collectives  94.1 us (23%)
  waiting for transfers between devices  75.2 us (18%)
  matrix products  58.2 us (14%)
  local copies, waits for them, and re-layouts  26.3 us (6%)
  other arithmetic  21.7 us (5%)
  loops' own time  12.8 us (3%)
    ppermute x22, starting transfers between devices, shifted(): return lax.ppermute(block, axis, route)  95 us
    ppermute x22, waiting for transfers between devices, shifted(): return lax.ppermute(block, axis, route)  65.4 us
    all_gather x11, blocking collectives, one_step(): lax.all_gather(forward_piece, 'pt', axis=1, tiled=True)  61.4 us
    dot_general x16, matrix products, add_rows(): jnp.dot(sent_part, kernel_rows(source_pts, source_norm, block_index), pre...  27 us
    ppermute x11, starting transfers between devices, take_series_all(): odd.append(lax.ppermute(odd[-1], 'pt', seen))  18.7 us
    dot_general x8, matrix products, ratio_part(): jnp.dot(fit_rows(block_index), inverse, precision=lax.Precision.HIGHEST)  13.8 us
    another operation x18, local copies, waits for them, and re-layouts  11.1 us
    ppermute x22, waiting for transfers between devices, take_series_all(): finding.append(lax.ppermute(finding[-1], 'pt', panels))  9.81 us
  transfers between devices with their start and end apart: 57, of which 33 were waited for; matrix products, arithmetic and copies ran while one was open for 2% of the time, Pallas kernels for 0%

profile of v1, /device:TPU:0, one launch (start us, length us, event | category | flops | bytes accessed | tf_op | source)
XLA Modules:
  0.0 411.7 jit_solution(5748715314064413350)
XLA Ops:
  0.7 7.6 %all_gather.22 = bf16[1,64,2048]{2,1,0:T(8,128)(2,1)S(1)} all-gather(bf16[1,64,512]{2,1,0:T(8,128)(2,1)} %param.20), channel_id=1, replica_groups=mesh['day'=8,'pt'=4] {'pt'}, dimensions={2}, use_global_device_ids=true | all-gather | bytes 327680 | tf_op jit(solution)/shard_map/all_gather | solution.py:63
  14.2 7.4 %all_gather.23 = f32[1,64,2048]{2,1,0:T(8,128)S(1)} all-gather(f32[1,64,512]{2,1,0:T(8,128)} %param.22), channel_id=1, replica_groups=mesh['day'=8,'pt'=4] {'pt'}, dimensions={2}, use_global_device_ids=true | all-gather | bytes 655360 | tf_op jit(solution)/shard_map/all_gather | solution.py:64
  30.0 312.2 %while.73 = (s32[]{:T(128)}, bf16[16,2048]{1,0:T(8,128)(2,1)S(1)}, bf16[16,2048]{1,0:T(8,128)(2,1)S(1)}, f32[64,512]{1,0:T(8,128)S(1)}, f32[64,512]{1,0:T(8,128)...) while((s32[]{:T(128)}, bf16[16,2048]{1,0:T(8,128)(2,1)S(1)}, ...), condition=%wide.region_14.15_spmd.clone.clone, body=%wide.region_3.14_spmd.clone.clone.sunk | while | flops 87085088 | bytes 3328036 | solution.py:173
  35.4 5.8 %all_gather.29 = f32[16,2048]{1,0:T(8,128)S(1)} all-gather(f32[16,512]{1,0:T(8,128)S(1)} %get-tuple-element.1379), channel_id=1, replica_groups=mesh['day'=8,'pt'=4] {'pt'}, dimensions={1}, use_global_device_ids=true | all-gather | bytes 163840 | tf_op jit(solution)/shard_map/while/body/eval_jaxpr/all_gather | solution.py:140
  57.4 5.7 %all_gather.29 = f32[16,2048]{1,0:T(8,128)S(1)} all-gather(f32[16,512]{1,0:T(8,128)S(1)} %get-tuple-element.1379), channel_id=1, replica_groups=mesh['day'=8,'pt'=4] {'pt'}, dimensions={1}, use_global_device_ids=true | all-gather | bytes 163840 | tf_op jit(solution)/shard_map/while/body/eval_jaxpr/all_gather | solution.py:140
  63.5 9.9 %collective-permute-start.3 = (bf16[16,2048]{1,0:T(8,128)(2,1)S(1)}, bf16[16,2048]{1,0:T(8,128)(2,1)S(1)}, u32[]{:S(2)}, u32[]{:S(2)}) collective-permute-start(bf16[16,2048]{1,0:T(8,128)(2,1)S(1)} %get-tuple-element.1384), channel_id=1, source_target_pairs={{0,4},{4,8},{8,12},{12,16},{16,20},{20,24},{24,28},{1,5},{5,9},{9,... | collective-permute-start | bytes 196616 | tf_op jit(solution)/shard_map/while/body/eval_jaxpr/ppermute | solution.py:43
  84.9 5.6 %all_gather.29 = f32[16,2048]{1,0:T(8,128)S(1)} all-gather(f32[16,512]{1,0:T(8,128)S(1)} %get-tuple-element.1379), channel_id=1, replica_groups=mesh['day'=8,'pt'=4] {'pt'}, dimensions={1}, use_global_device_ids=true | all-gather | bytes 163840 | tf_op jit(solution)/shard_map/while/body/eval_jaxpr/all_gather | solution.py:140
  90.9 9.3 %collective-permute-start.3 = (bf16[16,2048]{1,0:T(8,128)(2,1)S(1)}, bf16[16,2048]{1,0:T(8,128)(2,1)S(1)}, u32[]{:S(2)}, u32[]{:S(2)}) collective-permute-start(bf16[16,2048]{1,0:T(8,128)(2,1)S(1)} %get-tuple-element.1384), channel_id=1, source_target_pairs={{0,4},{4,8},{8,12},{12,16},{16,20},{20,24},{24,28},{1,5},{5,9},{9,... | collective-permute-start | bytes 196616 | tf_op jit(solution)/shard_map/while/body/eval_jaxpr/ppermute | solution.py:43
  111.8 5.5 %all_gather.29 = f32[16,2048]{1,0:T(8,128)S(1)} all-gather(f32[16,512]{1,0:T(8,128)S(1)} %get-tuple-element.1379), channel_id=1, replica_groups=mesh['day'=8,'pt'=4] {'pt'}, dimensions={1}, use_global_device_ids=true | all-gather | bytes 163840 | tf_op jit(solution)/shard_map/while/body/eval_jaxpr/all_gather | solution.py:140
  117.7 9.3 %collective-permute-start.3 = (bf16[16,2048]{1,0:T(8,128)(2,1)S(1)}, bf16[16,2048]{1,0:T(8,128)(2,1)S(1)}, u32[]{:S(2)}, u32[]{:S(2)}) collective-permute-start(bf16[16,2048]{1,0:T(8,128)(2,1)S(1)} %get-tuple-element.1384), channel_id=1, source_target_pairs={{0,4},{4,8},{8,12},{12,16},{16,20},{20,24},{24,28},{1,5},{5,9},{9,... | collective-permute-start | bytes 196616 | tf_op jit(solution)/shard_map/while/body/eval_jaxpr/ppermute | solution.py:43
  138.6 5.6 %all_gather.29 = f32[16,2048]{1,0:T(8,128)S(1)} all-gather(f32[16,512]{1,0:T(8,128)S(1)} %get-tuple-element.1379), channel_id=1, replica_groups=mesh['day'=8,'pt'=4] {'pt'}, dimensions={1}, use_global_device_ids=true | all-gather | bytes 163840 | tf_op jit(solution)/shard_map/while/body/eval_jaxpr/all_gather | solution.py:140
  144.5 9.3 %collective-permute-start.3 = (bf16[16,2048]{1,0:T(8,128)(2,1)S(1)}, bf16[16,2048]{1,0:T(8,128)(2,1)S(1)}, u32[]{:S(2)}, u32[]{:S(2)}) collective-permute-start(bf16[16,2048]{1,0:T(8,128)(2,1)S(1)} %get-tuple-element.1384), channel_id=1, source_target_pairs={{0,4},{4,8},{8,12},{12,16},{16,20},{20,24},{24,28},{1,5},{5,9},{9,... | collective-permute-start | bytes 196616 | tf_op jit(solution)/shard_map/while/body/eval_jaxpr/ppermute | solution.py:43
  171.3 11.0 %collective-permute-start.3 = (bf16[16,2048]{1,0:T(8,128)(2,1)S(1)}, bf16[16,2048]{1,0:T(8,128)(2,1)S(1)}, u32[]{:S(2)}, u32[]{:S(2)}) collective-permute-start(bf16[16,2048]{1,0:T(8,128)(2,1)S(1)} %get-tuple-element.1384), channel_id=1, source_target_pairs={{0,4},{4,8},{8,12},{12,16},{16,20},{20,24},{24,28},{1,5},{5,9},{9,... | collective-permute-start | bytes 196616 | tf_op jit(solution)/shard_map/while/body/eval_jaxpr/ppermute | solution.py:43
  184.2 17.1 %collective-permute-done.4 = bf16[16,2048]{1,0:T(8,128)(2,1)S(1)} collective-permute-done((bf16[16,2048]{1,0:T(8,128)(2,1)S(1)}, bf16[16,2048]{1,0:T(8,128)(2,1)S(1)}, u32[]{:S(2)}, u32[]{:S(2)}) %collective-permute-start.4) | collective-permute-done | bytes 65568 | tf_op jit(solution)/shard_map/while/body/eval_jaxpr/ppermute | solution.py:43
  206.7 5.6 %all_gather.29 = f32[16,2048]{1,0:T(8,128)S(1)} all-gather(f32[16,512]{1,0:T(8,128)S(1)} %get-tuple-element.1379), channel_id=1, replica_groups=mesh['day'=8,'pt'=4] {'pt'}, dimensions={1}, use_global_device_ids=true | all-gather | bytes 163840 | tf_op jit(solution)/shard_map/while/body/eval_jaxpr/all_gather | solution.py:140
  212.7 11.2 %collective-permute-start.3 = (bf16[16,2048]{1,0:T(8,128)(2,1)S(1)}, bf16[16,2048]{1,0:T(8,128)(2,1)S(1)}, u32[]{:S(2)}, u32[]{:S(2)}) collective-permute-start(bf16[16,2048]{1,0:T(8,128)(2,1)S(1)} %get-tuple-element.1384), channel_id=1, source_target_pairs={{0,4},{4,8},{8,12},{12,16},{16,20},{20,24},{24,28},{1,5},{5,9},{9,... | collective-permute-start | bytes 196616 | tf_op jit(solution)/shard_map/while/body/eval_jaxpr/ppermute | solution.py:43
  230.1 7.0 %conditional.8 = (f32[16,512]{1,0:T(8,128)}) conditional(s32[]{:T(128)} %convert_element_type.141, () %tuple.161, (bf16[16,2048]{1,0:T(8,128)(2,1)S(1)}, f32[2048]{0:T(1024)S(1)}, f32[512]{0:T(512)S(1)}, bf16[64,2048]{1,0:T(8,128)(2,1)S(1)}, bf16[64,512]{1,0:T(8,128)(2,1)S(1)}) %tuple.162), branch_computations={%region_9.9_spmd, %region_10.12_spmd} | conditional | flops 43270152 | bytes 222992 | solution.py:133
  230.1 7.0 %while.70 = (s32[]{:T(128)}, f32[16,512]{1,0:T(8,128)}, bf16[16,2048]{1,0:T(8,128)(2,1)S(1)}, f32[2048]{0:T(1024)S(1)}, f32[512]{0:T(512)S(1)}, /*index=5*/bf16[...) while((s32[]{:T(128)}, f32[16,512]{1,0:T(8,128)}, ...), condition=%wide.region_12.11_spmd.clone, body=%wide.region_11.10_spmd.clone.sunk | while | flops 43270152 | bytes 222888 | solution.py:102
  241.9 5.5 %all_gather.29 = f32[16,2048]{1,0:T(8,128)S(1)} all-gather(f32[16,512]{1,0:T(8,128)S(1)} %get-tuple-element.1379), channel_id=1, replica_groups=mesh['day'=8,'pt'=4] {'pt'}, dimensions={1}, use_global_device_ids=true | all-gather | bytes 163840 | tf_op jit(solution)/shard_map/while/body/eval_jaxpr/all_gather | solution.py:140
  247.8 7.5 %collective-permute-start.3 = (bf16[16,2048]{1,0:T(8,128)(2,1)S(1)}, bf16[16,2048]{1,0:T(8,128)(2,1)S(1)}, u32[]{:S(2)}, u32[]{:S(2)}) collective-permute-start(bf16[16,2048]{1,0:T(8,128)(2,1)S(1)} %get-tuple-element.1384), channel_id=1, source_target_pairs={{0,4},{4,8},{8,12},{12,16},{16,20},{20,24},{24,28},{1,5},{5,9},{9,... | collective-permute-start | bytes 196616 | tf_op jit(solution)/shard_map/while/body/eval_jaxpr/ppermute | solution.py:43
  261.4 7.1 %conditional.8 = (f32[16,512]{1,0:T(8,128)}) conditional(s32[]{:T(128)} %convert_element_type.141, () %tuple.161, (bf16[16,2048]{1,0:T(8,128)(2,1)S(1)}, f32[2048]{0:T(1024)S(1)}, f32[512]{0:T(512)S(1)}, bf16[64,2048]{1,0:T(8,128)(2,1)S(1)}, bf16[64,512]{1,0:T(8,128)(2,1)S(1)}) %tuple.162), branch_computations={%region_9.9_spmd, %region_10.12_spmd} | conditional | flops 43270152 | bytes 222992 | solution.py:133
  261.5 7.0 %while.70 = (s32[]{:T(128)}, f32[16,512]{1,0:T(8,128)}, bf16[16,2048]{1,0:T(8,128)(2,1)S(1)}, f32[2048]{0:T(1024)S(1)}, f32[512]{0:T(512)S(1)}, /*index=5*/bf16[...) while((s32[]{:T(128)}, f32[16,512]{1,0:T(8,128)}, ...), condition=%wide.region_12.11_spmd.clone, body=%wide.region_11.10_spmd.clone.sunk | while | flops 43270152 | bytes 222888 | solution.py:102
  273.3 5.6 %all_gather.29 = f32[16,2048]{1,0:T(8,128)S(1)} all-gather(f32[16,512]{1,0:T(8,128)S(1)} %get-tuple-element.1379), channel_id=1, replica_groups=mesh['day'=8,'pt'=4] {'pt'}, dimensions={1}, use_global_device_ids=true | all-gather | bytes 163840 | tf_op jit(solution)/shard_map/while/body/eval_jaxpr/all_gather | solution.py:140
  290.2 7.1 %conditional.8 = (f32[16,512]{1,0:T(8,128)}) conditional(s32[]{:T(128)} %convert_element_type.141, () %tuple.161, (bf16[16,2048]{1,0:T(8,128)(2,1)S(1)}, f32[2048]{0:T(1024)S(1)}, f32[512]{0:T(512)S(1)}, bf16[64,2048]{1,0:T(8,128)(2,1)S(1)}, bf16[64,512]{1,0:T(8,128)(2,1)S(1)}) %tuple.162), branch_computations={%region_9.9_spmd, %region_10.12_spmd} | conditional | flops 43270152 | bytes 222992 | solution.py:133
  290.2 7.1 %while.70 = (s32[]{:T(128)}, f32[16,512]{1,0:T(8,128)}, bf16[16,2048]{1,0:T(8,128)(2,1)S(1)}, f32[2048]{0:T(1024)S(1)}, f32[512]{0:T(512)S(1)}, /*index=5*/bf16[...) while((s32[]{:T(128)}, f32[16,512]{1,0:T(8,128)}, ...), condition=%wide.region_12.11_spmd.clone, body=%wide.region_11.10_spmd.clone.sunk | while | flops 43270152 | bytes 222888 | solution.py:102
  302.0 5.5 %all_gather.29 = f32[16,2048]{1,0:T(8,128)S(1)} all-gather(f32[16,512]{1,0:T(8,128)S(1)} %get-tuple-element.1379), channel_id=1, replica_groups=mesh['day'=8,'pt'=4] {'pt'}, dimensions={1}, use_global_device_ids=true | all-gather | bytes 163840 | tf_op jit(solution)/shard_map/while/body/eval_jaxpr/all_gather | solution.py:140
  317.0 7.0 %conditional.8 = (f32[16,512]{1,0:T(8,128)}) conditional(s32[]{:T(128)} %convert_element_type.141, () %tuple.161, (bf16[16,2048]{1,0:T(8,128)(2,1)S(1)}, f32[2048]{0:T(1024)S(1)}, f32[512]{0:T(512)S(1)}, bf16[64,2048]{1,0:T(8,128)(2,1)S(1)}, bf16[64,512]{1,0:T(8,128)(2,1)S(1)}) %tuple.162), branch_computations={%region_9.9_spmd, %region_10.12_spmd} | conditional | flops 43270152 | bytes 222992 | solution.py:133
  317.0 7.0 %while.70 = (s32[]{:T(128)}, f32[16,512]{1,0:T(8,128)}, bf16[16,2048]{1,0:T(8,128)(2,1)S(1)}, f32[2048]{0:T(1024)S(1)}, f32[512]{0:T(512)S(1)}, /*index=5*/bf16[...) while((s32[]{:T(128)}, f32[16,512]{1,0:T(8,128)}, ...), condition=%wide.region_12.11_spmd.clone, body=%wide.region_11.10_spmd.clone.sunk | while | flops 43270152 | bytes 222888 | solution.py:102
  328.8 5.5 %all_gather.29 = f32[16,2048]{1,0:T(8,128)S(1)} all-gather(f32[16,512]{1,0:T(8,128)S(1)} %get-tuple-element.1379), channel_id=1, replica_groups=mesh['day'=8,'pt'=4] {'pt'}, dimensions={1}, use_global_device_ids=true | all-gather | bytes 163840 | tf_op jit(solution)/shard_map/while/body/eval_jaxpr/all_gather | solution.py:140
  347.5 25.9 %while.71 = (s32[]{:T(128)}, f32[8,2048]{1,0:T(8,128)S(1)}, s32[8]{0:T(128)S(1)}, f32[2048]{0:T(1024)S(1)}, f32[2048]{0:T(1024)S(1)}, /*index=5*/f32[2048]{0:T(1...) while((s32[]{:T(128)}, f32[8,2048]{1,0:T(8,128)S(1)}, ...), condition=%wide.region_20.21_spmd, body=%wide.region_19.20_spmd.sunk | while | flops 75497480 | bytes 4528319 | solution.py:201
  374.7 29.2 %while.72 = (s32[]{:T(128)}, f32[8,256]{1,0:T(8,128)S(1)}, s32[8]{0:T(128)S(1)}, f32[2048]{0:T(1024)S(1)}, f32[2048]{0:T(1024)S(1)}, /*index=5*/bf16[64,2048]{1,...) while((s32[]{:T(128)}, f32[8,256]{1,0:T(8,128)S(1)}, ...), condition=%wide.region_23.24_spmd, body=%wide.region_22.23_spmd.sunk | while | flops 75497480 | bytes 4511931 | solution.py:210
  403.9 7.2 %all-reduce = f32[2048]{0:T(1024)S(1)} all-reduce(f32[2048]{0:T(1024)S(1)} %bitcast.86), channel_id=2, replica_groups=mesh['day'=8,'pt'=4] {'pt'}, use_global_device_ids=true, to_apply=%region_24.25.clone | all-reduce | flops 2048 | bytes 16384
  (460 shorter events, 244.4 us)
Async XLA Ops:
  8.3 21.4 %collective-permute-start.6 = (bf16[1,64,2048]{2,1,0:T(8,128)(2,1)S(1)}, bf16[1,64,2048]{2,1,0:T(8,128)(2,1)S(1)}, u32[]{:S(2)}, u32[]{:S(2)}) collective-permute-start(bf16[1,64,2048]{2,1,0:T(8,128)(2,1)S(1)} %all_gather.22), channel_id=1, source_target_pairs={{4,0},{8,4},{12,8},{16,12},{20,16},{24,20},{28,24},{5,1},{9,5},{13... | collective-permute-start | bytes 786440 | tf_op jit(solution)/shard_map/ppermute | solution.py:33
  9.5 20.2 %collective-permute-start.5 = (bf16[1,64,2048]{2,1,0:T(8,128)(2,1)S(1)}, bf16[1,64,2048]{2,1,0:T(8,128)(2,1)S(1)}, u32[]{:S(2)}, u32[]{:S(2)}) collective-permute-start(bf16[1,64,2048]{2,1,0:T(8,128)(2,1)S(1)} %all_gather.22), channel_id=1, source_target_pairs={{0,4},{4,8},{8,12},{12,16},{16,20},{20,24},{24,28},{1,5},{5,9},{9,... | collective-permute-start | bytes 786440 | tf_op jit(solution)/shard_map/ppermute | solution.py:31
  32.4 8.8 %collective-permute-start.2 = (f32[16,512]{1,0:T(8,128)S(1)}, f32[16,512]{1,0:T(8,128)S(1)}, u32[]{:S(2)}, u32[]{:S(2)}) collective-permute-start(f32[16,512]{1,0:T(8,128)S(1)} %get-tuple-element.1378), channel_id=1, source_target_pairs={{0,3},{1,0},{2,1},{3,2},{4,7},{5,4},{6,5},{7,6},{8,11},{9,8},{10,9... | collective-permute-start | bytes 98312 | tf_op jit(solution)/shard_map/while/body/eval_jaxpr/ppermute | solution.py:15
  41.5 6.2 %collective-permute-start.3 = (bf16[16,2048]{1,0:T(8,128)(2,1)S(1)}, bf16[16,2048]{1,0:T(8,128)(2,1)S(1)}, u32[]{:S(2)}, u32[]{:S(2)}) collective-permute-start(bf16[16,2048]{1,0:T(8,128)(2,1)S(1)} %get-tuple-element.1384), channel_id=1, source_target_pairs={{0,4},{4,8},{8,12},{12,16},{16,20},{20,24},{24,28},{1,5},{5,9},{9,... | collective-permute-start | bytes 196616 | tf_op jit(solution)/shard_map/while/body/eval_jaxpr/ppermute | solution.py:43
  45.8 6.2 %collective-permute-start.4 = (bf16[16,2048]{1,0:T(8,128)(2,1)S(1)}, bf16[16,2048]{1,0:T(8,128)(2,1)S(1)}, u32[]{:S(2)}, u32[]{:S(2)}) collective-permute-start(bf16[16,2048]{1,0:T(8,128)(2,1)S(1)} %get-tuple-element.1385), channel_id=1, source_target_pairs={{4,0},{8,4},{12,8},{16,12},{20,16},{24,20},{28,24},{5,1},{9,5},{13... | collective-permute-start | bytes 196616 | tf_op jit(solution)/shard_map/while/body/eval_jaxpr/ppermute | solution.py:43
  54.1 9.1 %collective-permute-start.2 = (f32[16,512]{1,0:T(8,128)S(1)}, f32[16,512]{1,0:T(8,128)S(1)}, u32[]{:S(2)}, u32[]{:S(2)}) collective-permute-start(f32[16,512]{1,0:T(8,128)S(1)} %get-tuple-element.1378), channel_id=1, source_target_pairs={{0,3},{1,0},{2,1},{3,2},{4,7},{5,4},{6,5},{7,6},{8,11},{9,8},{10,9... | collective-permute-start | bytes 98312 | tf_op jit(solution)/shard_map/while/body/eval_jaxpr/ppermute | solution.py:15
  63.5 11.8 %collective-permute-start.3 = (bf16[16,2048]{1,0:T(8,128)(2,1)S(1)}, bf16[16,2048]{1,0:T(8,128)(2,1)S(1)}, u32[]{:S(2)}, u32[]{:S(2)}) collective-permute-start(bf16[16,2048]{1,0:T(8,128)(2,1)S(1)} %get-tuple-element.1384), channel_id=1, source_target_pairs={{0,4},{4,8},{8,12},{12,16},{16,20},{20,24},{24,28},{1,5},{5,9},{9,... | collective-permute-start | bytes 196616 | tf_op jit(solution)/shard_map/while/body/eval_jaxpr/ppermute | solution.py:43
  73.4 6.2 %collective-permute-start.4 = (bf16[16,2048]{1,0:T(8,128)(2,1)S(1)}, bf16[16,2048]{1,0:T(8,128)(2,1)S(1)}, u32[]{:S(2)}, u32[]{:S(2)}) collective-permute-start(bf16[16,2048]{1,0:T(8,128)(2,1)S(1)} %get-tuple-element.1385), channel_id=1, source_target_pairs={{4,0},{8,4},{12,8},{16,12},{20,16},{24,20},{28,24},{5,1},{9,5},{13... | collective-permute-start | bytes 196616 | tf_op jit(solution)/shard_map/while/body/eval_jaxpr/ppermute | solution.py:43
  81.6 8.9 %collective-permute-start.2 = (f32[16,512]{1,0:T(8,128)S(1)}, f32[16,512]{1,0:T(8,128)S(1)}, u32[]{:S(2)}, u32[]{:S(2)}) collective-permute-start(f32[16,512]{1,0:T(8,128)S(1)} %get-tuple-element.1378), channel_id=1, source_target_pairs={{0,3},{1,0},{2,1},{3,2},{4,7},{5,4},{6,5},{7,6},{8,11},{9,8},{10,9... | collective-permute-start | bytes 98312 | tf_op jit(solution)/shard_map/while/body/eval_jaxpr/ppermute | solution.py:15
  90.9 11.2 %collective-permute-start.3 = (bf16[16,2048]{1,0:T(8,128)(2,1)S(1)}, bf16[16,2048]{1,0:T(8,128)(2,1)S(1)}, u32[]{:S(2)}, u32[]{:S(2)}) collective-permute-start(bf16[16,2048]{1,0:T(8,128)(2,1)S(1)} %get-tuple-element.1384), channel_id=1, source_target_pairs={{0,4},{4,8},{8,12},{12,16},{16,20},{20,24},{24,28},{1,5},{5,9},{9,... | collective-permute-start | bytes 196616 | tf_op jit(solution)/shard_map/while/body/eval_jaxpr/ppermute | solution.py:43
  100.2 6.2 %collective-permute-start.4 = (bf16[16,2048]{1,0:T(8,128)(2,1)S(1)}, bf16[16,2048]{1,0:T(8,128)(2,1)S(1)}, u32[]{:S(2)}, u32[]{:S(2)}) collective-permute-start(bf16[16,2048]{1,0:T(8,128)(2,1)S(1)} %get-tuple-element.1385), channel_id=1, source_target_pairs={{4,0},{8,4},{12,8},{16,12},{20,16},{24,20},{28,24},{5,1},{9,5},{13... | collective-permute-start | bytes 196616 | tf_op jit(solution)/shard_map/while/body/eval_jaxpr/ppermute | solution.py:43
  108.5 8.9 %collective-permute-start.2 = (f32[16,512]{1,0:T(8,128)S(1)}, f32[16,512]{1,0:T(8,128)S(1)}, u32[]{:S(2)}, u32[]{:S(2)}) collective-permute-start(f32[16,512]{1,0:T(8,128)S(1)} %get-tuple-element.1378), channel_id=1, source_target_pairs={{0,3},{1,0},{2,1},{3,2},{4,7},{5,4},{6,5},{7,6},{8,11},{9,8},{10,9... | collective-permute-start | bytes 98312 | tf_op jit(solution)/shard_map/while/body/eval_jaxpr/ppermute | solution.py:15
  117.7 11.2 %collective-permute-start.3 = (bf16[16,2048]{1,0:T(8,128)(2,1)S(1)}, bf16[16,2048]{1,0:T(8,128)(2,1)S(1)}, u32[]{:S(2)}, u32[]{:S(2)}) collective-permute-start(bf16[16,2048]{1,0:T(8,128)(2,1)S(1)} %get-tuple-element.1384), channel_id=1, source_target_pairs={{0,4},{4,8},{8,12},{12,16},{16,20},{20,24},{24,28},{1,5},{5,9},{9,... | collective-permute-start | bytes 196616 | tf_op jit(solution)/shard_map/while/body/eval_jaxpr/ppermute | solution.py:43
  135.3 8.9 %collective-permute-start.2 = (f32[16,512]{1,0:T(8,128)S(1)}, f32[16,512]{1,0:T(8,128)S(1)}, u32[]{:S(2)}, u32[]{:S(2)}) collective-permute-start(f32[16,512]{1,0:T(8,128)S(1)} %get-tuple-element.1378), channel_id=1, source_target_pairs={{0,3},{1,0},{2,1},{3,2},{4,7},{5,4},{6,5},{7,6},{8,11},{9,8},{10,9... | collective-permute-start | bytes 98312 | tf_op jit(solution)/shard_map/while/body/eval_jaxpr/ppermute | solution.py:15
  144.5 11.2 %collective-permute-start.3 = (bf16[16,2048]{1,0:T(8,128)(2,1)S(1)}, bf16[16,2048]{1,0:T(8,128)(2,1)S(1)}, u32[]{:S(2)}, u32[]{:S(2)}) collective-permute-start(bf16[16,2048]{1,0:T(8,128)(2,1)S(1)} %get-tuple-element.1384), channel_id=1, source_target_pairs={{0,4},{4,8},{8,12},{12,16},{16,20},{20,24},{24,28},{1,5},{5,9},{9,... | collective-permute-start | bytes 196616 | tf_op jit(solution)/shard_map/while/body/eval_jaxpr/ppermute | solution.py:43
  153.9 6.2 %collective-permute-start.4 = (bf16[16,2048]{1,0:T(8,128)(2,1)S(1)}, bf16[16,2048]{1,0:T(8,128)(2,1)S(1)}, u32[]{:S(2)}, u32[]{:S(2)}) collective-permute-start(bf16[16,2048]{1,0:T(8,128)(2,1)S(1)} %get-tuple-element.1385), channel_id=1, source_target_pairs={{4,0},{8,4},{12,8},{16,12},{20,16},{24,20},{28,24},{5,1},{9,5},{13... | collective-permute-start | bytes 196616 | tf_op jit(solution)/shard_map/while/body/eval_jaxpr/ppermute | solution.py:43
  162.1 8.9 %collective-permute-start.2 = (f32[16,512]{1,0:T(8,128)S(1)}, f32[16,512]{1,0:T(8,128)S(1)}, u32[]{:S(2)}, u32[]{:S(2)}) collective-permute-start(f32[16,512]{1,0:T(8,128)S(1)} %get-tuple-element.1378), channel_id=1, source_target_pairs={{0,3},{1,0},{2,1},{3,2},{4,7},{5,4},{6,5},{7,6},{8,11},{9,8},{10,9... | collective-permute-start | bytes 98312 | tf_op jit(solution)/shard_map/while/body/eval_jaxpr/ppermute | solution.py:15
  171.3 12.9 %collective-permute-start.3 = (bf16[16,2048]{1,0:T(8,128)(2,1)S(1)}, bf16[16,2048]{1,0:T(8,128)(2,1)S(1)}, u32[]{:S(2)}, u32[]{:S(2)}) collective-permute-start(bf16[16,2048]{1,0:T(8,128)(2,1)S(1)} %get-tuple-element.1384), channel_id=1, source_target_pairs={{0,4},{4,8},{8,12},{12,16},{16,20},{20,24},{24,28},{1,5},{5,9},{9,... | collective-permute-start | bytes 196616 | tf_op jit(solution)/shard_map/while/body/eval_jaxpr/ppermute | solution.py:43
  182.3 19.0 %collective-permute-start.4 = (bf16[16,2048]{1,0:T(8,128)(2,1)S(1)}, bf16[16,2048]{1,0:T(8,128)(2,1)S(1)}, u32[]{:S(2)}, u32[]{:S(2)}) collective-permute-start(bf16[16,2048]{1,0:T(8,128)(2,1)S(1)} %get-tuple-element.1385), channel_id=1, source_target_pairs={{4,0},{8,4},{12,8},{16,12},{20,16},{24,20},{28,24},{5,1},{9,5},{13... | collective-permute-start | bytes 196616 | tf_op jit(solution)/shard_map/while/body/eval_jaxpr/ppermute | solution.py:43
  203.4 9.0 %collective-permute-start.2 = (f32[16,512]{1,0:T(8,128)S(1)}, f32[16,512]{1,0:T(8,128)S(1)}, u32[]{:S(2)}, u32[]{:S(2)}) collective-permute-start(f32[16,512]{1,0:T(8,128)S(1)} %get-tuple-element.1378), channel_id=1, source_target_pairs={{0,3},{1,0},{2,1},{3,2},{4,7},{5,4},{6,5},{7,6},{8,11},{9,8},{10,9... | collective-permute-start | bytes 98312 | tf_op jit(solution)/shard_map/while/body/eval_jaxpr/ppermute | solution.py:15
  212.7 13.1 %collective-permute-start.3 = (bf16[16,2048]{1,0:T(8,128)(2,1)S(1)}, bf16[16,2048]{1,0:T(8,128)(2,1)S(1)}, u32[]{:S(2)}, u32[]{:S(2)}) collective-permute-start(bf16[16,2048]{1,0:T(8,128)(2,1)S(1)} %get-tuple-element.1384), channel_id=1, source_target_pairs={{0,4},{4,8},{8,12},{12,16},{16,20},{20,24},{24,28},{1,5},{5,9},{9,... | collective-permute-start | bytes 196616 | tf_op jit(solution)/shard_map/while/body/eval_jaxpr/ppermute | solution.py:43
  223.9 6.2 %collective-permute-start.4 = (bf16[16,2048]{1,0:T(8,128)(2,1)S(1)}, bf16[16,2048]{1,0:T(8,128)(2,1)S(1)}, u32[]{:S(2)}, u32[]{:S(2)}) collective-permute-start(bf16[16,2048]{1,0:T(8,128)(2,1)S(1)} %get-tuple-element.1385), channel_id=1, source_target_pairs={{4,0},{8,4},{12,8},{16,12},{20,16},{24,20},{28,24},{5,1},{9,5},{13... | collective-permute-start | bytes 196616 | tf_op jit(solution)/shard_map/while/body/eval_jaxpr/ppermute | solution.py:43
  238.6 8.9 %collective-permute-start.2 = (f32[16,512]{1,0:T(8,128)S(1)}, f32[16,512]{1,0:T(8,128)S(1)}, u32[]{:S(2)}, u32[]{:S(2)}) collective-permute-start(f32[16,512]{1,0:T(8,128)S(1)} %get-tuple-element.1378), channel_id=1, source_target_pairs={{0,3},{1,0},{2,1},{3,2},{4,7},{5,4},{6,5},{7,6},{8,11},{9,8},{10,9... | collective-permute-start | bytes 98312 | tf_op jit(solution)/shard_map/while/body/eval_jaxpr/ppermute | solution.py:15
  247.8 9.4 %collective-permute-start.3 = (bf16[16,2048]{1,0:T(8,128)(2,1)S(1)}, bf16[16,2048]{1,0:T(8,128)(2,1)S(1)}, u32[]{:S(2)}, u32[]{:S(2)}) collective-permute-start(bf16[16,2048]{1,0:T(8,128)(2,1)S(1)} %get-tuple-element.1384), channel_id=1, source_target_pairs={{0,4},{4,8},{8,12},{12,16},{16,20},{20,24},{24,28},{1,5},{5,9},{9,... | collective-permute-start | bytes 196616 | tf_op jit(solution)/shard_map/while/body/eval_jaxpr/ppermute | solution.py:43
  255.3 6.2 %collective-permute-start.4 = (bf16[16,2048]{1,0:T(8,128)(2,1)S(1)}, bf16[16,2048]{1,0:T(8,128)(2,1)S(1)}, u32[]{:S(2)}, u32[]{:S(2)}) collective-permute-start(bf16[16,2048]{1,0:T(8,128)(2,1)S(1)} %get-tuple-element.1385), channel_id=1, source_target_pairs={{4,0},{8,4},{12,8},{16,12},{20,16},{24,20},{28,24},{5,1},{9,5},{13... | collective-permute-start | bytes 196616 | tf_op jit(solution)/shard_map/while/body/eval_jaxpr/ppermute | solution.py:43
  269.9 9.0 %collective-permute-start.2 = (f32[16,512]{1,0:T(8,128)S(1)}, f32[16,512]{1,0:T(8,128)S(1)}, u32[]{:S(2)}, u32[]{:S(2)}) collective-permute-start(f32[16,512]{1,0:T(8,128)S(1)} %get-tuple-element.1378), channel_id=1, source_target_pairs={{0,3},{1,0},{2,1},{3,2},{4,7},{5,4},{6,5},{7,6},{8,11},{9,8},{10,9... | collective-permute-start | bytes 98312 | tf_op jit(solution)/shard_map/while/body/eval_jaxpr/ppermute | solution.py:15
  279.2 6.6 %collective-permute-start.3 = (bf16[16,2048]{1,0:T(8,128)(2,1)S(1)}, bf16[16,2048]{1,0:T(8,128)(2,1)S(1)}, u32[]{:S(2)}, u32[]{:S(2)}) collective-permute-start(bf16[16,2048]{1,0:T(8,128)(2,1)S(1)} %get-tuple-element.1384), channel_id=1, source_target_pairs={{0,4},{4,8},{8,12},{12,16},{16,20},{20,24},{24,28},{1,5},{5,9},{9,... | collective-permute-start | bytes 196616 | tf_op jit(solution)/shard_map/while/body/eval_jaxpr/ppermute | solution.py:43
  284.0 6.2 %collective-permute-start.4 = (bf16[16,2048]{1,0:T(8,128)(2,1)S(1)}, bf16[16,2048]{1,0:T(8,128)(2,1)S(1)}, u32[]{:S(2)}, u32[]{:S(2)}) collective-permute-start(bf16[16,2048]{1,0:T(8,128)(2,1)S(1)} %get-tuple-element.1385), channel_id=1, source_target_pairs={{4,0},{8,4},{12,8},{16,12},{20,16},{24,20},{28,24},{5,1},{9,5},{13... | collective-permute-start | bytes 196616 | tf_op jit(solution)/shard_map/while/body/eval_jaxpr/ppermute | solution.py:43
  298.7 8.9 %collective-permute-start.2 = (f32[16,512]{1,0:T(8,128)S(1)}, f32[16,512]{1,0:T(8,128)S(1)}, u32[]{:S(2)}, u32[]{:S(2)}) collective-permute-start(f32[16,512]{1,0:T(8,128)S(1)} %get-tuple-element.1378), channel_id=1, source_target_pairs={{0,3},{1,0},{2,1},{3,2},{4,7},{5,4},{6,5},{7,6},{8,11},{9,8},{10,9... | collective-permute-start | bytes 98312 | tf_op jit(solution)/shard_map/while/body/eval_jaxpr/ppermute | solution.py:15
  310.8 6.2 %collective-permute-start.4 = (bf16[16,2048]{1,0:T(8,128)(2,1)S(1)}, bf16[16,2048]{1,0:T(8,128)(2,1)S(1)}, u32[]{:S(2)}, u32[]{:S(2)}) collective-permute-start(bf16[16,2048]{1,0:T(8,128)(2,1)S(1)} %get-tuple-element.1385), channel_id=1, source_target_pairs={{4,0},{8,4},{12,8},{16,12},{20,16},{24,20},{28,24},{5,1},{9,5},{13... | collective-permute-start | bytes 196616 | tf_op jit(solution)/shard_map/while/body/eval_jaxpr/ppermute | solution.py:43
  325.4 8.9 %collective-permute-start.2 = (f32[16,512]{1,0:T(8,128)S(1)}, f32[16,512]{1,0:T(8,128)S(1)}, u32[]{:S(2)}, u32[]{:S(2)}) collective-permute-start(f32[16,512]{1,0:T(8,128)S(1)} %get-tuple-element.1378), channel_id=1, source_target_pairs={{0,3},{1,0},{2,1},{3,2},{4,7},{5,4},{6,5},{7,6},{8,11},{9,8},{10,9... | collective-permute-start | bytes 98312 | tf_op jit(solution)/shard_map/while/body/eval_jaxpr/ppermute | solution.py:15
  336.0 6.2 %collective-permute-start.4 = (bf16[16,2048]{1,0:T(8,128)(2,1)S(1)}, bf16[16,2048]{1,0:T(8,128)(2,1)S(1)}, u32[]{:S(2)}, u32[]{:S(2)}) collective-permute-start(bf16[16,2048]{1,0:T(8,128)(2,1)S(1)} %get-tuple-element.1385), channel_id=1, source_target_pairs={{4,0},{8,4},{12,8},{16,12},{20,16},{24,20},{28,24},{5,1},{9,5},{13... | collective-permute-start | bytes 196616 | tf_op jit(solution)/shard_map/while/body/eval_jaxpr/ppermute | solution.py:43
  (32 other events, 831.2 us)
